TPU v7x, 32 devices: a whole 2x2x4 slice. The times are simulated.
32 devices in a mesh: gx: 8 (over z, x), gy: 4 (over y, core).
Axes of the slice: x: 2, y: 2, z: 4, core: 2. Of those that a mesh axis runs over, the one named last changes fastest.
Arguments:
- patches: bfloat16 [128, 64, 256], P('gx', 'gy'), may hold values from -9 to 9
- w_query: bfloat16 [256, 256], replicated, may hold values from -2 to 2
- w_key: bfloat16 [256, 256], replicated, may hold values from -2 to 2
- w_value: bfloat16 [256, 256], replicated, may hold values from -0.375 to 0.375
- w_out: bfloat16 [256, 256], replicated, may hold values from -0.375 to 0.375
- region_memory: bfloat16 [8, 4, 4, 64, 512], P('gx', 'gy'), may hold values from -6 to 6
- region_owner: int32 [8, 4, 4, 2], P('gx', 'gy'), may hold values from 0 to 7, all different within a row; in each aligned block of 4 rows (0 to 3, 4 to 7, ..., all dimensions but the last counted through in order) at most 2 rows name the same one
- region_local: int32 [8, 4, 4, 2], P('gx', 'gy'), may hold values from 0 to 3
- grad_out: bfloat16 [128, 64, 256], P('gx', 'gy'), may hold values from -6 to 6
Outputs:
- layer_out: bfloat16 [128, 64, 256], P('gx', 'gy')
- grad_patches: bfloat16 [128, 64, 256], P('gx', 'gy')
- grad_w_query: float32 [256, 256], replicated
- grad_w_key: float32 [256, 256], replicated
- grad_w_value: float32 [256, 256], replicated
- grad_w_out: float32 [256, 256], replicated
Inputs may be any that keep to these rules, and one draw needn't show every extreme that they name: `region_owner`: each block names two different owner tiles. The blocks of one tile name one owner at most 2 times, a bound that some tile reaches.
All inputs are finite; a program needn't handle non-finite values.
Results may differ from a plain program's by a relative error of at most 0.02.
Values may be sent and summed in bfloat16 or wider, within the bound.
No kernel may reach another device: no remote copies, remote signals or barrier semaphores. Data moves between devices by JAX's collectives and lax.ppermute only.
A program may use at most 64 MiB of HBM per device.

v0:
```python
import math
import jax
import jax.numpy as jnp
from jax import lax
from jax.sharding import PartitionSpec as P

D = 256
HEADS = 2
HEAD_DIM = 128
BSIDE = 8
BT = 64
masked_score = -1000000000.0


def padded(block, sides, width):
    for axis, dim in sides:
        count = lax.axis_size(axis)
        forward = [(i, i + 1) for i in range(count - 1)]
        backward = [(target, source) for source, target in forward]
        low = lax.ppermute(
            lax.slice_in_dim(block, block.shape[dim] - width, None, axis=dim), axis, forward
        )
        high = lax.ppermute(lax.slice_in_dim(block, 0, width, axis=dim), axis, backward)
        block = jnp.concatenate([low, block, high], axis=dim)
    return block


def to_blocks(grid_array):
    grid_rows, grid_cols, feature_width = grid_array.shape
    shaped = grid_array.reshape(grid_rows // BSIDE, BSIDE, grid_cols // BSIDE, BSIDE, feature_width)
    return shaped.transpose(0, 2, 1, 3, 4).reshape(
        grid_rows // BSIDE, grid_cols // BSIDE, BSIDE * BSIDE, feature_width
    )


def from_blocks(block_array):
    block_rows, block_cols, block_tokens, feature_width = block_array.shape
    shaped = block_array.reshape(block_rows, block_cols, BSIDE, BSIDE, feature_width)
    return shaped.transpose(0, 2, 1, 3, 4).reshape(
        block_rows * BSIDE, block_cols * BSIDE, feature_width
    )


def split_heads(source):
    return source.reshape(source.shape[:-1] + (HEADS, source.shape[-1] // HEADS))


def key_pieces(keyval_pad, key_valid, region_keyval):
    block_rows, block_cols = (region_keyval.shape[0], region_keyval.shape[1])
    pieces = []
    for row_off in range(3):
        for col_off in range(3):
            key_block = keyval_pad[row_off : row_off + block_rows, col_off : col_off + block_cols]
            valid_mask = key_valid[row_off : row_off + block_rows, col_off : col_off + block_cols]
            pieces.append((key_block[..., :D], key_block[..., D:], valid_mask))
    merged = region_keyval.reshape(block_rows, block_cols, 2 * BT, 2 * D)
    pieces.append(
        (merged[..., :D], merged[..., D:], jnp.ones((block_rows, block_cols), dtype=jnp.bool_))
    )
    return pieces


def piece_scores(query_heads, key_part, valid_mask):
    scores = jnp.einsum(
        "abqhe,abkhe->abhqk", query_heads, split_heads(key_part), preferred_element_type=jnp.float32
    )
    scores = scores * (1.0 / math.sqrt(HEAD_DIM))
    return jnp.where(valid_mask[:, :, None, None, None], scores, masked_score)


def attend_forward(query_blocks, keyval_pad, key_valid, region_keyval):
    query_heads = split_heads(query_blocks)
    pieces = key_pieces(keyval_pad, key_valid, region_keyval)
    scores = [
        piece_scores(query_heads, key_part, valid_mask)
        for key_part, value_part, valid_mask in pieces
    ]
    row_top = jnp.max(jnp.concatenate(scores, -1), -1, keepdims=True)
    row_total = sum(
        (jnp.sum(jnp.exp(part_scores - row_top), -1, keepdims=True) for part_scores in scores)
    )
    log_total = row_top + jnp.log(row_total)
    mixed_sum = jnp.zeros(query_heads.shape, jnp.float32)
    for part_scores, (key_part, value_part, valid_mask) in zip(scores, pieces):
        weights = jnp.exp(part_scores - log_total).astype(jnp.bfloat16)
        mixed_sum = mixed_sum + jnp.einsum(
            "abhqk,abkhe->abqhe",
            weights,
            split_heads(value_part),
            preferred_element_type=jnp.float32,
        )
    output = mixed_sum.reshape(query_blocks.shape).astype(jnp.bfloat16)
    return (output, log_total[..., 0])


def query_grads(
    query_blocks, keyval_pad, key_valid, region_keyval, log_total, dout_blocks, delta_rows
):
    query_heads = split_heads(query_blocks)
    dout_heads = split_heads(dout_blocks)
    accum_sum = jnp.zeros(query_heads.shape, jnp.float32)
    for key_part, value_part, valid_mask in key_pieces(keyval_pad, key_valid, region_keyval):
        part_scores = piece_scores(query_heads, key_part, valid_mask)
        prob_part = jnp.exp(part_scores - log_total[..., None])
        grad_prob = jnp.einsum(
            "abqhe,abkhe->abhqk",
            dout_heads,
            split_heads(value_part),
            preferred_element_type=jnp.float32,
        )
        grad_score = (prob_part * (grad_prob - delta_rows[..., None])).astype(jnp.bfloat16)
        accum_sum = accum_sum + jnp.einsum(
            "abhqk,abkhe->abqhe",
            grad_score,
            split_heads(key_part),
            preferred_element_type=jnp.float32,
        )
    return (
        (accum_sum * (1.0 / math.sqrt(HEAD_DIM))).reshape(query_blocks.shape).astype(jnp.bfloat16)
    )


def key_grads(keyval_center, query_pad, dout_pad, log_pad, delta_pad, query_valid):
    block_rows, block_cols = (keyval_center.shape[0], keyval_center.shape[1])
    key_heads = split_heads(keyval_center[..., :D])
    value_heads = split_heads(keyval_center[..., D:])
    grad_key = jnp.zeros(key_heads.shape, jnp.float32)
    grad_value = jnp.zeros(key_heads.shape, jnp.float32)
    for row_off in range(3):
        for col_off in range(3):
            query_heads = split_heads(
                query_pad[row_off : row_off + block_rows, col_off : col_off + block_cols]
            )
            dout_heads = split_heads(
                dout_pad[row_off : row_off + block_rows, col_off : col_off + block_cols]
            )
            log_part = log_pad[row_off : row_off + block_rows, col_off : col_off + block_cols]
            delta_part = delta_pad[row_off : row_off + block_rows, col_off : col_off + block_cols]
            valid_mask = query_valid[row_off : row_off + block_rows, col_off : col_off + block_cols]
            part_scores = jnp.einsum(
                "abqhe,abkhe->abhqk", query_heads, key_heads, preferred_element_type=jnp.float32
            )
            part_scores = part_scores * (1.0 / math.sqrt(HEAD_DIM))
            prob_part = jnp.where(
                valid_mask[:, :, None, None, None], jnp.exp(part_scores - log_part[..., None]), 0.0
            )
            grad_prob = jnp.einsum(
                "abqhe,abkhe->abhqk", dout_heads, value_heads, preferred_element_type=jnp.float32
            )
            grad_score = (prob_part * (grad_prob - delta_part[..., None])).astype(jnp.bfloat16)
            grad_key = grad_key + jnp.einsum(
                "abhqk,abqhe->abkhe", grad_score, query_heads, preferred_element_type=jnp.float32
            )
            rounded_prob = prob_part.astype(jnp.bfloat16)
            grad_value = grad_value + jnp.einsum(
                "abhqk,abqhe->abkhe", rounded_prob, dout_heads, preferred_element_type=jnp.float32
            )
    out_shape = (block_rows, block_cols, BT, D)
    grad_key = (grad_key * (1.0 / math.sqrt(HEAD_DIM))).reshape(out_shape).astype(jnp.bfloat16)
    return (grad_key, grad_value.reshape(out_shape).astype(jnp.bfloat16))


def inner_rows(left_rows, right_rows):
    return lax.dot_general(
        left_rows, right_rows, (((0,), (0,)), ((), ())), preferred_element_type=jnp.float32
    )


def on_device(
    patches, w_query, w_key, w_value, w_out, region_memory, region_owner, region_local, grad_out
):
    tile_rows, tile_cols, model_width = patches.shape
    block_rows, block_cols = (tile_rows // BSIDE, tile_cols // BSIDE)
    block_count = block_rows * block_cols
    flat_in = patches.reshape(-1, model_width)
    w_pair = jnp.concatenate([w_key, w_value], 1)
    queries = jnp.dot(flat_in, w_query, preferred_element_type=jnp.float32).astype(jnp.bfloat16)
    keyvals = jnp.dot(flat_in, w_pair, preferred_element_type=jnp.float32).astype(jnp.bfloat16)
    keyvals = keyvals.reshape(tile_rows, tile_cols, 2 * model_width)
    keyval_grid = padded(keyvals, (("gx", 0), ("gy", 1)), BSIDE)
    keyval_pad = to_blocks(keyval_grid)
    gx_count = lax.axis_size("gx")
    gy_count = lax.axis_size("gy")
    row_ids = lax.axis_index("gx") * block_rows - 1 + jnp.arange(block_rows + 2, dtype=jnp.int32)
    col_ids = lax.axis_index("gy") * block_cols - 1 + jnp.arange(block_cols + 2, dtype=jnp.int32)
    row_valid = (row_ids >= 0) & (row_ids < block_rows * gx_count)
    col_valid = (col_ids >= 0) & (col_ids < block_cols * gy_count)
    key_valid = row_valid[:, None] & col_valid[None, :]
    owners = region_owner.reshape(2 * block_count)
    local_ids = region_local.reshape(2 * block_count)
    memory_local = region_memory.reshape(
        region_memory.shape[2], region_memory.shape[3], region_memory.shape[4]
    )
    region_count = memory_local.shape[0]
    row_tables = lax.all_gather(memory_local, "gx", axis=0, tiled=True)
    fetched = jnp.take(row_tables, owners * region_count + local_ids, axis=0)
    region_keyval = fetched.reshape(
        block_rows, block_cols, 2, memory_local.shape[1], memory_local.shape[2]
    )
    query_blocks = to_blocks(queries.reshape(tile_rows, tile_cols, model_width))
    outputs, log_totals = attend_forward(query_blocks, keyval_pad, key_valid, region_keyval)
    attended = from_blocks(outputs).reshape(-1, model_width)
    layer_out = jnp.dot(attended, w_out, preferred_element_type=jnp.float32).astype(jnp.bfloat16)
    grad_flat = grad_out.reshape(-1, model_width)
    d_attended = jnp.dot(grad_flat, w_out.T, preferred_element_type=jnp.float32).astype(
        jnp.bfloat16
    )
    grad_out_local = inner_rows(attended, grad_flat)
    dout_blocks = to_blocks(d_attended.reshape(tile_rows, tile_cols, model_width))
    delta_rows = jnp.sum(
        split_heads(dout_blocks).astype(jnp.float32) * split_heads(outputs).astype(jnp.float32), -1
    )
    delta_rows = delta_rows.transpose(0, 1, 3, 2)
    d_queries = query_grads(
        query_blocks, keyval_pad, key_valid, region_keyval, log_totals, dout_blocks, delta_rows
    )
    query_grid = jnp.concatenate(
        [
            queries.reshape(tile_rows, tile_cols, model_width),
            d_attended.reshape(tile_rows, tile_cols, model_width),
        ],
        -1,
    )
    query_halo = padded(query_grid, (("gx", 0), ("gy", 1)), BSIDE)
    stat_grid = from_blocks(jnp.concatenate([log_totals, delta_rows], 2).transpose(0, 1, 3, 2))
    stat_halo = padded(stat_grid, (("gx", 0), ("gy", 1)), BSIDE)
    query_all = to_blocks(query_halo)
    stat_pad = to_blocks(stat_halo).transpose(0, 1, 3, 2)
    d_keys, d_values = key_grads(
        keyval_pad[1:-1, 1:-1],
        query_all[..., :model_width],
        query_all[..., model_width:],
        stat_pad[:, :, :HEADS],
        stat_pad[:, :, HEADS:],
        key_valid,
    )
    dq_flat = from_blocks(d_queries).reshape(-1, model_width)
    dk_flat = from_blocks(d_keys).reshape(-1, model_width)
    dv_flat = from_blocks(d_values).reshape(-1, model_width)
    grads_joined = jnp.concatenate([dq_flat, dk_flat, dv_flat], 1)
    w_stacked = jnp.concatenate([w_query.T, w_key.T, w_value.T], 0)
    grad_patches = jnp.dot(grads_joined, w_stacked, preferred_element_type=jnp.float32).astype(
        jnp.bfloat16
    )
    summed = lax.psum(
        (
            inner_rows(flat_in, dq_flat),
            inner_rows(flat_in, dk_flat),
            inner_rows(flat_in, dv_flat),
            grad_out_local,
        ),
        ("gx", "gy"),
    )
    return (
        layer_out.reshape(tile_rows, tile_cols, model_width),
        grad_patches.reshape(tile_rows, tile_cols, model_width),
        summed[0],
        summed[1],
        summed[2],
        summed[3],
    )


def solution(mesh):
    return jax.shard_map(
        on_device,
        mesh=mesh,
        in_specs=(
            P("gx", "gy", None),
            P(),
            P(),
            P(),
            P(),
            P("gx", "gy", None, None, None),
            P("gx", "gy", None, None),
            P("gx", "gy", None, None),
            P("gx", "gy", None),
        ),
        out_specs=(P("gx", "gy", None), P("gx", "gy", None), P(), P(), P(), P()),
        check_vma=False,
    )
```

profile of v0, /device:TPU:0, one launch (start us, length us, event | category | flops | bytes accessed | tf_op | source)
XLA Modules:
  0.0 271.7 jit_solution(11771590287470757042)
XLA Ops:
  8.1 1.2 convolution_convert_fusion
  9.3 1.3 collective-permute-start.1
  10.6 5.5 %collective-permute-start = (bf16[8,16,512]{2,1,0:T(8,128)(2,1)S(1)}, bf16[8,16,512]{2,1,0:T(8,128)(2,1)S(1)}, u32[]{:S(2)}, u32[]{:S(2)}) collective-permute-start(bf16[8,16,512]{2,1,0:T(8,128)(2,1)S(1)} %bitcast.503), channel_id=1, source_target_pairs={{0,4},{4,8},{8,12},{12,16},{16,20},{20,24},{24,28},{1,5},{5,9},{9,... | collective-permute-start | bytes 393224 | tf_op jit(solution)/shard_map/ppermute | solution.py:20
  16.1 1.1 convolution_convert_fusion.4
  17.2 1.2 convolution_convert_fusion.2
  18.4 4.8 %collective-permute-start.4 = (bf16[8,16,512]{2,1,0:T(8,128)(2,1)S(1)}, bf16[8,16,512]{2,1,0:T(8,128)(2,1)S(1)}, u32[]{:S(2)}, u32[]{:S(2)}) collective-permute-start(bf16[8,16,512]{2,1,0:T(8,128)(2,1)S(1)} %get-tuple-element.85), channel_id=1, source_target_pairs={{0,4},{4,8},{8,12},{12,16},{16,20},{20,24},{24,28},{1,5},{5,9},{9,... | collective-permute-start | bytes 393224 | tf_op jit(solution)/shard_map/ppermute | solution.py:20
  23.2 1.3 collective-permute-start.5
  25.1 3.5 %collective-permute-done.4 = bf16[8,16,512]{2,1,0:T(8,128)(2,1)S(1)} collective-permute-done((bf16[8,16,512]{2,1,0:T(8,128)(2,1)S(1)}, bf16[8,16,512]{2,1,0:T(8,128)(2,1)S(1)}, u32[]{:S(2)}, u32[]{:S(2)}) %collective-permute-start.4) | collective-permute-done | bytes 131104 | tf_op jit(solution)/shard_map/ppermute | solution.py:20
  28.6 1.5 collective-permute-done.5
  30.2 1.3 collective-permute-start.6
  31.5 1.3 collective-permute-start.7
  33.0 4.8 %collective-permute-start.2 = (bf16[32,8,512]{2,1,0:T(8,128)(2,1)S(1)}, bf16[32,8,512]{2,1,0:T(8,128)(2,1)S(1)}, u32[]{:S(2)}, u32[]{:S(2)}) collective-permute-start(bf16[32,8,512]{2,1,0:T(8,128)(2,1)S(1)} %get-tuple-element.83), channel_id=1, source_target_pairs={{0,1},{1,2},{2,3},{4,5},{5,6},{6,7},{8,9},{9,10},{10,11},{12,13},{... | collective-permute-start | bytes 786440 | tf_op jit(solution)/shard_map/ppermute | solution.py:20
  37.7 1.3 collective-permute-start.3
  39.7 2.8 %collective-permute-done.3 = bf16[32,8,512]{2,1,0:T(8,128)(2,1)} collective-permute-done((bf16[32,8,512]{2,1,0:T(8,128)(2,1)S(1)}, bf16[32,8,512]{2,1,0:T(8,128)(2,1)}, u32[]{:S(2)}, u32[]{:S(2)}) %collective-permute-start.3) | collective-permute-done | bytes 262176 | tf_op jit(solution)/shard_map/ppermute | solution.py:23
  42.5 1.1 pad_maximum_fusion
  43.7 1.2 slice_bitcast_fusion.18
  50.2 1.5 slice_bitcast_fusion
  51.7 13.7 %all-gather.3.cloned.1.call-done = bf16[1,1,32,64,512]{4,3,1,0,2:T(8,128)(2,1)} async-done(((bf16[1,1,4,64,512]{4,3,1,0,2:T(8,128)(2,1)}), bf16[1,1,32,64,512]{4,3,1,0,2:T(8,128)(2,1)}) %all-gather.3.cloned.1.call-update) | async-done | bytes 2097168 | tf_op jit(solution)/shard_map/all_gather | solution.py:195
  65.4 2.2 gather_fusion
  68.1 1.2 fusion.445
  70.9 1.2 fusion.118
  74.2 1.0 multiply_reduce_fusion
  75.2 2.1 fusion.84
  77.3 2.2 convolution_add_fusion.24
  79.5 2.2 convolution_add_fusion.23
  81.7 1.4 convolution_add_fusion.22
  83.2 1.3 convolution_add_fusion.21
  84.5 1.3 convolution_add_fusion.20
  85.9 1.3 convolution_add_fusion.19
  88.7 2.4 collective-permute-start.8
  93.0 1.3 collective-permute-start.9
  94.3 4.7 %collective-permute-done.9 = f32[8,16,4]{1,0,2:T(8,128)S(1)} collective-permute-done((f32[8,16,4]{1,0,2:T(8,128)S(1)}, f32[8,16,4]{1,0,2:T(8,128)S(1)}, u32[]{:S(2)}, u32[]{:S(2)}) %collective-permute-start.9) | collective-permute-done | bytes 2080 | tf_op jit(solution)/shard_map/ppermute | solution.py:23
  99.0 1.3 collective-permute-start.10
  100.3 1.5 collective-permute-start.11
  102.8 2.4 collective-permute-done.11
  111.9 1.6 convert_element_type.219
  113.5 1.6 copy.530
  115.1 2.0 convolution_add_fusion.15
  117.1 1.3 convolution_add_fusion.14
  118.5 1.3 convolution_add_fusion.13
  119.7 1.3 convolution_add_fusion.12
  121.0 1.2 convolution_add_fusion.11
  126.3 1.0 convolution_convert_fusion.1
  127.3 130.5 %all-reduce.3.cloned.1.call-done = (f32[256,256]{0,1:T(8,128)}, f32[256,256]{0,1:T(8,128)}, f32[256,256]{0,1:T(8,128)}, f32[256,256]{1,0:T(8,128)}) async-done(((f32[256,256]{0,1:T(8,128)}, f32[256,256]{0,1:T(8,128)}, f32[256,256]{0,1:T(8,128)}, f32[256,256]{1,0:T(8,128)}), (f32[256,256]{0,1:T(8,128)}, f32[256,256]{0,1:T(8,128)}, f32[256,256]{0,1:T(8,128)}, ...) | async-done | bytes 1048592 | tf_op jit(solution)/shard_map/psum | solution.py:245
  257.8 1.8 copy.531
  259.6 1.8 copy.532
  261.4 1.8 copy.533
  263.2 1.7 copy.1109
  (278 shorter events, 25.6 us)
Async XLA Ops:
  7.2 17.4 %copy-start.59 = (s32[1,1,4,2]{2,3,1,0:T(2,128)S(1)}, s32[1,1,4,2]{2,3,1,0:T(2,128)}, u32[]{:S(2)}) copy-start(s32[1,1,4,2]{2,3,1,0:T(2,128)} %param.16) | copy-start | bytes 100
  7.2 17.4 %copy-start.60 = (s32[1,1,4,2]{2,3,1,0:T(2,128)S(1)}, s32[1,1,4,2]{2,3,1,0:T(2,128)}, u32[]{:S(2)}) copy-start(s32[1,1,4,2]{2,3,1,0:T(2,128)} %param.15) | copy-start | bytes 100
  7.2 58.2 %all-gather.3.cloned.1.call-start = ((), (), s32[]{:S(2)}) async-start(), calls=%async_computation | async-start | bytes 2359296 | tf_op jit(solution)/shard_map/all_gather | solution.py:195
  7.9 249.9 %all-reduce.3.cloned.1.call-start = ((), (), s32[]{:S(2)}) async-start(), calls=%async_computation.1 | async-start | bytes 2097152 | tf_op jit(solution)/shard_map/psum | solution.py:245
  9.3 23.5 %collective-permute-start.1 = (bf16[8,16,512]{2,1,0:T(8,128)(2,1)S(1)}, bf16[8,16,512]{2,1,0:T(8,128)(2,1)S(1)}, u32[]{:S(2)}, u32[]{:S(2)}) collective-permute-start(bf16[8,16,512]{2,1,0:T(8,128)(2,1)S(1)} %bitcast.504), channel_id=1, source_target_pairs={{4,0},{8,4},{12,8},{16,12},{20,16},{24,20},{28,24},{5,1},{9,5},{13... | collective-permute-start | bytes 393224 | tf_op jit(solution)/shard_map/ppermute | solution.py:23
  10.6 22.2 %collective-permute-start = (bf16[8,16,512]{2,1,0:T(8,128)(2,1)S(1)}, bf16[8,16,512]{2,1,0:T(8,128)(2,1)S(1)}, u32[]{:S(2)}, u32[]{:S(2)}) collective-permute-start(bf16[8,16,512]{2,1,0:T(8,128)(2,1)S(1)} %bitcast.503), channel_id=1, source_target_pairs={{0,4},{4,8},{8,12},{12,16},{16,20},{20,24},{24,28},{1,5},{5,9},{9,... | collective-permute-start | bytes 393224 | tf_op jit(solution)/shard_map/ppermute | solution.py:20
  18.4 10.2 %collective-permute-start.4 = (bf16[8,16,512]{2,1,0:T(8,128)(2,1)S(1)}, bf16[8,16,512]{2,1,0:T(8,128)(2,1)S(1)}, u32[]{:S(2)}, u32[]{:S(2)}) collective-permute-start(bf16[8,16,512]{2,1,0:T(8,128)(2,1)S(1)} %get-tuple-element.85), channel_id=1, source_target_pairs={{0,4},{4,8},{8,12},{12,16},{16,20},{20,24},{24,28},{1,5},{5,9},{9,... | collective-permute-start | bytes 393224 | tf_op jit(solution)/shard_map/ppermute | solution.py:20
  23.2 6.9 %collective-permute-start.5 = (bf16[8,16,512]{2,1,0:T(8,128)(2,1)S(1)}, bf16[8,16,512]{2,1,0:T(8,128)(2,1)S(1)}, u32[]{:S(2)}, u32[]{:S(2)}) collective-permute-start(bf16[8,16,512]{2,1,0:T(8,128)(2,1)S(1)} %get-tuple-element.86), channel_id=1, source_target_pairs={{4,0},{8,4},{12,8},{16,12},{20,16},{24,20},{28,24},{5,1},{9,5},{13... | collective-permute-start | bytes 393224 | tf_op jit(solution)/shard_map/ppermute | solution.py:23
  25.0 20.0 %copy-start.75 = (pred[2,2]{1,0:T(4,128)(4,1)}, pred[2,2]{1,0:T(4,128)(4,1)S(1)}, u32[]{:S(2)}) copy-start(pred[2,2]{1,0:T(4,128)(4,1)S(1)} %get-tuple-element.112) | copy-start | bytes 16
  25.0 20.3 %copy-start.73 = (pred[2,2]{1,0:T(4,128)(4,1)}, pred[2,2]{1,0:T(4,128)(4,1)S(1)}, u32[]{:S(2)}) copy-start(pred[2,2]{1,0:T(4,128)(4,1)S(1)} %get-tuple-element.113) | copy-start | bytes 16
  25.0 20.5 %copy-start.71 = (pred[2,2]{1,0:T(4,128)(4,1)}, pred[2,2]{1,0:T(4,128)(4,1)S(1)}, u32[]{:S(2)}) copy-start(pred[2,2]{1,0:T(4,128)(4,1)S(1)} %get-tuple-element.114) | copy-start | bytes 16
  25.0 20.7 %copy-start.69 = (pred[2,2]{1,0:T(4,128)(4,1)}, pred[2,2]{1,0:T(4,128)(4,1)S(1)}, u32[]{:S(2)}) copy-start(pred[2,2]{1,0:T(4,128)(4,1)S(1)} %get-tuple-element.115) | copy-start | bytes 16
  25.0 20.9 %copy-start.65 = (pred[2,2]{1,0:T(4,128)(4,1)}, pred[2,2]{1,0:T(4,128)(4,1)S(1)}, u32[]{:S(2)}) copy-start(pred[2,2]{1,0:T(4,128)(4,1)S(1)} %get-tuple-element.117) | copy-start | bytes 16
  25.0 21.8 %copy-start.63 = (pred[2,2]{1,0:T(4,128)(4,1)}, pred[2,2]{1,0:T(4,128)(4,1)S(1)}, u32[]{:S(2)}) copy-start(pred[2,2]{1,0:T(4,128)(4,1)S(1)} %get-tuple-element.118) | copy-start | bytes 16
  25.1 22.6 %copy-start.61 = (pred[2,2]{1,0:T(4,128)(4,1)}, pred[2,2]{1,0:T(4,128)(4,1)S(1)}, u32[]{:S(2)}) copy-start(pred[2,2]{1,0:T(4,128)(4,1)S(1)} %get-tuple-element.111) | copy-start | bytes 16
  25.1 23.4 %copy-start.77 = (pred[2,2]{1,0:T(4,128)(4,1)}, pred[2,2]{1,0:T(4,128)(4,1)S(1)}, u32[]{:S(2)}) copy-start(pred[2,2]{1,0:T(4,128)(4,1)S(1)} %get-tuple-element.119) | copy-start | bytes 16
  25.1 24.3 %copy-start.67 = (pred[2,2]{1,0:T(4,128)(4,1)}, pred[2,2]{1,0:T(4,128)(4,1)S(1)}, u32[]{:S(2)}) copy-start(pred[2,2]{1,0:T(4,128)(4,1)S(1)} %get-tuple-element.116) | copy-start | bytes 16
  30.2 9.3 %collective-permute-start.6 = (bf16[32,8,512]{2,1,0:T(8,128)(2,1)S(1)}, bf16[32,8,512]{2,1,0:T(8,128)(2,1)S(1)}, u32[]{:S(2)}, u32[]{:S(2)}) collective-permute-start(bf16[32,8,512]{2,1,0:T(8,128)(2,1)S(1)} %get-tuple-element.79), channel_id=1, source_target_pairs={{0,1},{1,2},{2,3},{4,5},{5,6},{6,7},{8,9},{9,10},{10,11},{12,13},{... | collective-permute-start | bytes 786440 | tf_op jit(solution)/shard_map/ppermute | solution.py:20
  31.5 8.0 %collective-permute-start.7 = (bf16[32,8,512]{2,1,0:T(8,128)(2,1)S(1)}, bf16[32,8,512]{2,1,0:T(8,128)(2,1)S(1)}, u32[]{:S(2)}, u32[]{:S(2)}) collective-permute-start(bf16[32,8,512]{2,1,0:T(8,128)(2,1)S(1)} %get-tuple-element.80), channel_id=1, source_target_pairs={{1,0},{2,1},{3,2},{5,4},{6,5},{7,6},{9,8},{10,9},{11,10},{13,12},{... | collective-permute-start | bytes 786440 | tf_op jit(solution)/shard_map/ppermute | solution.py:23
  33.0 6.8 %collective-permute-start.2 = (bf16[32,8,512]{2,1,0:T(8,128)(2,1)S(1)}, bf16[32,8,512]{2,1,0:T(8,128)(2,1)S(1)}, u32[]{:S(2)}, u32[]{:S(2)}) collective-permute-start(bf16[32,8,512]{2,1,0:T(8,128)(2,1)S(1)} %get-tuple-element.83), channel_id=1, source_target_pairs={{0,1},{1,2},{2,3},{4,5},{5,6},{6,7},{8,9},{9,10},{10,11},{12,13},{... | collective-permute-start | bytes 786440 | tf_op jit(solution)/shard_map/ppermute | solution.py:20
  37.7 4.8 %collective-permute-start.3 = (bf16[32,8,512]{2,1,0:T(8,128)(2,1)S(1)}, bf16[32,8,512]{2,1,0:T(8,128)(2,1)}, u32[]{:S(2)}, u32[]{:S(2)}) collective-permute-start(bf16[32,8,512]{2,1,0:T(8,128)(2,1)S(1)} %get-tuple-element.84), channel_id=1, source_target_pairs={{1,0},{2,1},{3,2},{5,4},{6,5},{7,6},{9,8},{10,9},{11,10},{13,12},{... | collective-permute-start | bytes 786440 | tf_op jit(solution)/shard_map/ppermute | solution.py:23
  39.4 9.9 %copy-start.48 = (bf16[2,2,64,2,128]{4,3,2,1,0:T(2,128)(2,1)}, bf16[2,2,64,2,128]{4,3,2,1,0:T(2,128)(2,1)S(1)}, u32[]{:S(2)}) copy-start(bf16[2,2,64,2,128]{4,3,2,1,0:T(2,128)(2,1)S(1)} %reshape_reshape.29) | copy-start | bytes 393220
  44.9 4.3 %copy-start.38 = (bf16[2,2,8,2,8,128]{5,4,3,2,1,0:T(8,128)(2,1)}, bf16[2,2,8,2,8,128]{5,4,3,2,1,0:T(8,128)(2,1)S(1)}, u32[]{:S(2)}) copy-start(bf16[2,2,8,2,8,128]{5,4,3,2,1,0:T(8,128)(2,1)S(1)} %get-tuple-element.69) | copy-start | bytes 393220
  45.0 4.3 %copy-start.40 = (bf16[2,2,8,2,8,128]{5,4,3,2,1,0:T(8,128)(2,1)}, bf16[2,2,8,2,8,128]{5,4,3,2,1,0:T(8,128)(2,1)S(1)}, u32[]{:S(2)}) copy-start(bf16[2,2,8,2,8,128]{5,4,3,2,1,0:T(8,128)(2,1)S(1)} %get-tuple-element.70) | copy-start | bytes 393220
  45.0 4.3 %copy-start.42 = (bf16[2,2,8,2,8,128]{5,4,3,2,1,0:T(8,128)(2,1)}, bf16[2,2,8,2,8,128]{5,4,3,2,1,0:T(8,128)(2,1)S(1)}, u32[]{:S(2)}) copy-start(bf16[2,2,8,2,8,128]{5,4,3,2,1,0:T(8,128)(2,1)S(1)} %get-tuple-element.71) | copy-start | bytes 393220
  45.0 4.3 %copy-start.43 = (bf16[2,2,8,2,8,128]{5,4,3,2,1,0:T(8,128)(2,1)}, bf16[2,2,8,2,8,128]{5,4,3,2,1,0:T(8,128)(2,1)S(1)}, u32[]{:S(2)}) copy-start(bf16[2,2,8,2,8,128]{5,4,3,2,1,0:T(8,128)(2,1)S(1)} %get-tuple-element.72) | copy-start | bytes 393220
  45.0 4.3 %copy-start.44 = (bf16[2,2,8,2,8,128]{5,4,3,2,1,0:T(8,128)(2,1)}, bf16[2,2,8,2,8,128]{5,4,3,2,1,0:T(8,128)(2,1)S(1)}, u32[]{:S(2)}) copy-start(bf16[2,2,8,2,8,128]{5,4,3,2,1,0:T(8,128)(2,1)S(1)} %get-tuple-element.74) | copy-start | bytes 393220
  45.0 4.3 %copy-start.45 = (bf16[2,2,8,2,8,128]{5,4,3,2,1,0:T(8,128)(2,1)}, bf16[2,2,8,2,8,128]{5,4,3,2,1,0:T(8,128)(2,1)S(1)}, u32[]{:S(2)}) copy-start(bf16[2,2,8,2,8,128]{5,4,3,2,1,0:T(8,128)(2,1)S(1)} %get-tuple-element.75) | copy-start | bytes 393220
  45.0 4.3 %copy-start.46 = (bf16[2,2,8,2,8,128]{5,4,3,2,1,0:T(8,128)(2,1)}, bf16[2,2,8,2,8,128]{5,4,3,2,1,0:T(8,128)(2,1)S(1)}, u32[]{:S(2)}) copy-start(bf16[2,2,8,2,8,128]{5,4,3,2,1,0:T(8,128)(2,1)S(1)} %get-tuple-element.76) | copy-start | bytes 393220
  45.0 4.3 %copy-start.47 = (bf16[2,2,8,2,8,128]{5,4,3,2,1,0:T(8,128)(2,1)}, bf16[2,2,8,2,8,128]{5,4,3,2,1,0:T(8,128)(2,1)S(1)}, u32[]{:S(2)}) copy-start(bf16[2,2,8,2,8,128]{5,4,3,2,1,0:T(8,128)(2,1)S(1)} %get-tuple-element.77) | copy-start | bytes 393220
  45.0 4.3 %copy-start.32 = (bf16[2,2,8,2,8,128]{5,4,3,2,1,0:T(8,128)(2,1)}, bf16[2,2,8,2,8,128]{5,4,3,2,1,0:T(8,128)(2,1)S(1)}, u32[]{:S(2)}) copy-start(bf16[2,2,8,2,8,128]{5,4,3,2,1,0:T(8,128)(2,1)S(1)} %get-tuple-element.73) | copy-start | bytes 393220
  77.3 4.5 %copy-start.18 = (bf16[2,2,8,2,8,128]{5,4,3,2,1,0:T(8,128)(2,1)S(1)}, bf16[2,2,8,2,8,128]{5,4,3,2,1,0:T(8,128)(2,1)}, u32[]{:S(2)}) copy-start(bf16[2,2,8,2,8,128]{5,4,3,2,1,0:T(8,128)(2,1)} %get-tuple-element.66) | copy-start | bytes 393220
  79.5 5.0 %copy-start.16 = (bf16[2,2,8,2,8,128]{5,4,3,2,1,0:T(8,128)(2,1)S(1)}, bf16[2,2,8,2,8,128]{5,4,3,2,1,0:T(8,128)(2,1)}, u32[]{:S(2)}) copy-start(bf16[2,2,8,2,8,128]{5,4,3,2,1,0:T(8,128)(2,1)} %get-tuple-element.64) | copy-start | bytes 393220
  79.5 6.4 %copy-start.14 = (bf16[2,2,8,2,8,128]{5,4,3,2,1,0:T(8,128)(2,1)S(1)}, bf16[2,2,8,2,8,128]{5,4,3,2,1,0:T(8,128)(2,1)}, u32[]{:S(2)}) copy-start(bf16[2,2,8,2,8,128]{5,4,3,2,1,0:T(8,128)(2,1)} %get-tuple-element.63) | copy-start | bytes 393220
  81.7 5.5 %copy-start.12 = (bf16[2,2,8,2,8,128]{5,4,3,2,1,0:T(8,128)(2,1)S(1)}, bf16[2,2,8,2,8,128]{5,4,3,2,1,0:T(8,128)(2,1)}, u32[]{:S(2)}) copy-start(bf16[2,2,8,2,8,128]{5,4,3,2,1,0:T(8,128)(2,1)} %get-tuple-element.62) | copy-start | bytes 393220
  83.2 4.5 %copy-start.10 = (bf16[2,2,8,2,8,128]{5,4,3,2,1,0:T(8,128)(2,1)S(1)}, bf16[2,2,8,2,8,128]{5,4,3,2,1,0:T(8,128)(2,1)}, u32[]{:S(2)}) copy-start(bf16[2,2,8,2,8,128]{5,4,3,2,1,0:T(8,128)(2,1)} %get-tuple-element.61) | copy-start | bytes 393220
  88.7 5.5 %collective-permute-start.8 = (f32[8,16,4]{1,0,2:T(8,128)S(1)}, f32[8,16,4]{1,0,2:T(8,128)S(1)}, u32[]{:S(2)}, u32[]{:S(2)}) collective-permute-start(f32[8,16,4]{1,0,2:T(8,128)S(1)} %slice.401), channel_id=1, source_target_pairs={{0,4},{4,8},{8,12},{12,16},{16,20},{20,24},{24,28},{1,5},{5,9},{9,... | collective-permute-start | bytes 6152 | tf_op jit(solution)/shard_map/ppermute | solution.py:20
  91.4 14.9 %copy-start.33 = (bf16[2,2,8,2,8,128]{5,4,3,2,1,0:T(8,128)(2,1)S(1)}, bf16[2,2,8,2,8,128]{5,4,3,2,1,0:T(8,128)(2,1)}, u32[]{:S(2)}) copy-start(bf16[2,2,8,2,8,128]{5,4,3,2,1,0:T(8,128)(2,1)} %copy-done.32) | copy-start | bytes 393220
  91.5 14.9 %copy-start.37 = (bf16[2,2,8,2,8,128]{5,4,3,2,1,0:T(8,128)(2,1)S(1)}, bf16[2,2,8,2,8,128]{5,4,3,2,1,0:T(8,128)(2,1)}, u32[]{:S(2)}) copy-start(bf16[2,2,8,2,8,128]{5,4,3,2,1,0:T(8,128)(2,1)} %get-tuple-element.60) | copy-start | bytes 393220
  91.5 14.9 %copy-start.78 = (pred[2,2]{1,0:T(4,128)(4,1)S(1)}, pred[2,2]{1,0:T(4,128)(4,1)}, u32[]{:S(2)}) copy-start(pred[2,2]{1,0:T(4,128)(4,1)} %copy-done.77) | copy-start | bytes 16
  92.5 14.1 %copy-start.8 = (bf16[2,2,8,2,8,128]{5,4,3,2,1,0:T(8,128)(2,1)S(1)}, bf16[2,2,8,2,8,128]{5,4,3,2,1,0:T(8,128)(2,1)}, u32[]{:S(2)}) copy-start(bf16[2,2,8,2,8,128]{5,4,3,2,1,0:T(8,128)(2,1)} %get-tuple-element.59) | copy-start | bytes 393220
  92.7 13.8 %copy-start.50 = (bf16[2,8,2,8,256]{4,3,2,1,0:T(8,128)(2,1)}, bf16[2,8,2,8,256]{4,3,2,1,0:T(8,128)(2,1)S(1)}, u32[]{:S(2)}) copy-start(bf16[2,8,2,8,256]{4,3,2,1,0:T(8,128)(2,1)S(1)} %copy.449) | copy-start | bytes 393220
  93.0 6.0 %collective-permute-start.9 = (f32[8,16,4]{1,0,2:T(8,128)S(1)}, f32[8,16,4]{1,0,2:T(8,128)S(1)}, u32[]{:S(2)}, u32[]{:S(2)}) collective-permute-start(f32[8,16,4]{1,0,2:T(8,128)S(1)} %slice.403), channel_id=1, source_target_pairs={{4,0},{8,4},{12,8},{16,12},{20,16},{24,20},{28,24},{5,1},{9,5},{13... | collective-permute-start | bytes 6152 | tf_op jit(solution)/shard_map/ppermute | solution.py:23
  99.0 3.7 %collective-permute-start.10 = (f32[32,8,4]{1,0,2:T(8,128)S(1)}, f32[32,8,4]{1,0,2:T(8,128)S(1)}, u32[]{:S(2)}, u32[]{:S(2)}) collective-permute-start(f32[32,8,4]{1,0,2:T(8,128)S(1)} %get-tuple-element.89), channel_id=1, source_target_pairs={{0,1},{1,2},{2,3},{4,5},{5,6},{6,7},{8,9},{9,10},{10,11},{12,13},{... | collective-permute-start | bytes 12296 | tf_op jit(solution)/shard_map/ppermute | solution.py:20
  100.3 4.8 %collective-permute-start.11 = (f32[32,8,4]{1,0,2:T(8,128)S(1)}, f32[32,8,4]{1,0,2:T(8,128)S(1)}, u32[]{:S(2)}, u32[]{:S(2)}) collective-permute-start(f32[32,8,4]{1,0,2:T(8,128)S(1)} %get-tuple-element.90), channel_id=1, source_target_pairs={{1,0},{2,1},{3,2},{5,4},{6,5},{7,6},{9,8},{10,9},{11,10},{13,12},{... | collective-permute-start | bytes 12296 | tf_op jit(solution)/shard_map/ppermute | solution.py:23
  101.8 5.3 %copy-start.53 = (bf16[2,2,8,2,8,128]{5,4,3,2,1,0:T(8,128)(2,1)S(1)}, bf16[2,2,8,2,8,128]{5,4,3,2,1,0:T(8,128)(2,1)}, u32[]{:S(2)}) copy-start(bf16[2,2,8,2,8,128]{5,4,3,2,1,0:T(8,128)(2,1)} %get-tuple-element.44) | copy-start | bytes 393220
  101.8 5.3 %copy-start.76 = (pred[2,2]{1,0:T(4,128)(4,1)S(1)}, pred[2,2]{1,0:T(4,128)(4,1)}, u32[]{:S(2)}) copy-start(pred[2,2]{1,0:T(4,128)(4,1)} %copy-done.75) | copy-start | bytes 16
  110.5 6.6 %copy-start.23 = (f32[2,2,2,64,64]{3,4,2,1,0:T(8,128)S(1)}, f32[2,2,2,64,64]{3,4,2,1,0:T(8,128)}, u32[]{:S(2)}) copy-start(f32[2,2,2,64,64]{3,4,2,1,0:T(8,128)} %copy-done.22) | copy-start | bytes 393220
  (45 other events, 95.9 us)
Sparse Core Ops, SparseCore 0:
  10.2 55.1 all-gather.2
  125.6 132.2 all-reduce.2
where the time goes:
time: 273 us; the launch traced here: 272 us
  waiting for transfers between devices  160 us (59%)
  matrix products  44.2 us (16%)
  starting transfers between devices  28.1 us (10%)
  local copies, waits for them, and re-layouts  20.5 us (8%)
  between operations  15.9 us (6%)
  other arithmetic  3.19 us (1%)
    psum x1, waiting for transfers between devices, on_device(): lax.psum((inner_rows(flat_in, dq_flat), inner_rows(flat_in, dk_flat), inn...  131 us
    ppermute x6, starting transfers between devices, padded(): lax.ppermute(lax.slice_in_dim(block, block.shape[dim] - width, None, axis...  20.1 us
    all_gather x1, waiting for transfers between devices, on_device(): row_tables = lax.all_gather(memory_local, 'gx', axis=0, tiled=True)  13.7 us
    dot_general x10, matrix products, query_grads(): jnp.einsum('abhqk,abkhe->abqhe', grad_score, split_heads(key_part), prefe...  13.1 us
    ppermute x6, waiting for transfers between devices, padded(): lax.ppermute(lax.slice_in_dim(block, 0, width, axis=dim), axis, backward)  11.4 us
    unnamed x166, local copies, waits for them, and re-layouts  10.8 us
    dot_general x9, matrix products, key_grads(): jnp.einsum('abhqk,abqhe->abkhe', grad_score, query_heads, preferred_eleme...  8.38 us
    ppermute x6, starting transfers between devices, padded(): lax.ppermute(lax.slice_in_dim(block, 0, width, axis=dim), axis, backward)  7.92 us
  transfers between devices with their start and end apart: 14, of which 7 were waited for; matrix products, arithmetic and copies ran while one was open for 7% of the time, Pallas kernels for 0%

commit v1 on v0

--- a/solution.py
+++ b/solution.py
@@ -10,6 +10,28 @@
 BSIDE = 8
 BT = 64
 masked_score = -1000000000.0
+
+
+def in_order(parts, dim):
+    parts = jnp.moveaxis(parts, 0, dim)
+    shape = parts.shape
+    return parts.reshape(*shape[:dim], shape[dim] * shape[dim + 1], *shape[dim + 2 :])
+
+
+def ring_gather(array, axis, dim):
+    size = lax.axis_size(axis)
+    pairs = [(i, (i + 1) % size) for i in range(size)]
+    back = [(b, a) for a, b in pairs]
+    lower, upper = ([], [])
+    for lap in range(size - 1):
+        if lap % 2 == 0:
+            lower.append(lax.ppermute(lower[-1] if lower else array, axis, pairs))
+        else:
+            upper.append(lax.ppermute(upper[-1] if upper else array, axis, back))
+    blocks = jnp.stack([*lower[::-1], array, *upper])
+    shift = lax.axis_index(axis) - len(lower)
+    blocks = blocks[(jnp.arange(size) - shift) % size]
+    return in_order(blocks, dim)
 
 
 def padded(block, sides, width):
@@ -192,7 +214,7 @@
         region_memory.shape[2], region_memory.shape[3], region_memory.shape[4]
     )
     region_count = memory_local.shape[0]
-    row_tables = lax.all_gather(memory_local, "gx", axis=0, tiled=True)
+    row_tables = ring_gather(memory_local, "gx", 0)
     fetched = jnp.take(row_tables, owners * region_count + local_ids, axis=0)
     region_keyval = fetched.reshape(
         block_rows, block_cols, 2, memory_local.shape[1], memory_local.shape[2]

time: 273 us -> 301 us (1.10)
  matrix products: 44.2 us -> 58.9 us
  starting transfers between devices: 28.1 us -> 41.4 us
  waiting for transfers between devices: 160 us -> 152 us
  local copies, waits for them, and re-layouts: 20.5 us -> 28.3 us
    ppermute x0 -> x7, starting transfers between devices: none -> 19.1 us  [the longest x3 9.73 us: ring_gather(): upper.append(lax.ppermute(upper[-1] if upper else array, axis, back))]
    all_gather x1 -> x0, waiting for transfers between devices: 13.7 us -> none  [on_device(): row_tables = lax.all_gather(memory_local, 'gx', axis=0, tiled=True)]
    ppermute x0 -> x7, waiting for transfers between devices: none -> 11.3 us  [the longest x4 11.3 us: ring_gather(): lower.append(lax.ppermute(lower[-1] if lower else array, axis, pairs))]
    dot_general x9, matrix products: 8.38 us -> 16.7 us  [key_grads(): jnp.einsum('abhqk,abqhe->abkhe', grad_score, query_heads, preferred_eleme...]
    ppermute x6, starting transfers between devices: 20.1 us -> 14.4 us  [padded(): lax.ppermute(lax.slice_in_dim(block, block.shape[dim] - width, None, axis...]
    unnamed x166 -> x181, local copies, waits for them, and re-layouts: 10.8 us -> 15.9 us
    dot_general x10, matrix products: 6.23 us -> 10.5 us  [piece_scores(): jnp.einsum('abqhe,abkhe->abhqk', query_heads, split_heads(key_part), pref...]
    ppermute x6, waiting for transfers between devices: 11.4 us -> 8.01 us  [padded(): lax.ppermute(lax.slice_in_dim(block, 0, width, axis=dim), axis, backward)]
  transfers between devices with their start and end apart: 14 -> 20, of which waited for: 7 -> 7; matrix products, arithmetic and copies ran while one was open for 7% -> 9% of each run, Pallas kernels for 0% -> 0%
where the time goes in v1:
time: 301 us; the launch traced here: 300 us
  waiting for transfers between devices  152 us (50%)
  matrix products  58.9 us (20%)
  starting transfers between devices  41.4 us (14%)
  local copies, waits for them, and re-layouts  28.3 us (9%)
  between operations  15.7 us (5%)
  other arithmetic  3.45 us (1%)
    psum x1, waiting for transfers between devices, on_device(): lax.psum((inner_rows(flat_in, dq_flat), inner_rows(flat_in, dk_flat), inn...  130 us
    dot_general x9, matrix products, key_grads(): jnp.einsum('abhqk,abqhe->abkhe', grad_score, query_heads, preferred_eleme...  16.7 us
    unnamed x181, local copies, waits for them, and re-layouts  15.9 us
    ppermute x6, starting transfers between devices, padded(): lax.ppermute(lax.slice_in_dim(block, block.shape[dim] - width, None, axis...  14.4 us
    dot_general x10, matrix products, query_grads(): jnp.einsum('abhqk,abkhe->abqhe', grad_score, split_heads(key_part), prefe...  13.1 us
    ppermute x4, waiting for transfers between devices, ring_gather(): lower.append(lax.ppermute(lower[-1] if lower else array, axis, pairs))  11.3 us
    dot_general x10, matrix products, piece_scores(): jnp.einsum('abqhe,abkhe->abhqk', query_heads, split_heads(key_part), pref...  10.5 us
    ppermute x3, starting transfers between devices, ring_gather(): upper.append(lax.ppermute(upper[-1] if upper else array, axis, back))  9.73 us
  transfers between devices with their start and end apart: 20, of which 7 were waited for; matrix products, arithmetic and copies ran while one was open for 9% of the time, Pallas kernels for 0%

profile of v1, /device:TPU:0, one launch (start us, length us, event | category | flops | bytes accessed | tf_op | source)
XLA Modules:
  0.0 300.1 jit_solution(463458870912633536)
XLA Ops:
  7.2 3.0 collective-permute-start.4
  10.2 3.1 %collective-permute-start.8 = (bf16[4,64,512]{2,1,0:T(8,128)(2,1)}, bf16[4,64,512]{2,1,0:T(8,128)(2,1)S(1)}, u32[]{:S(2)}, u32[]{:S(2)}) collective-permute-start(bf16[4,64,512]{2,1,0:T(8,128)(2,1)} %bitcast.517), channel_id=1, source_target_pairs={{4,0},{8,4},{12,8},{16,12},{20,16},{24,20},{28,24},{0,28},{5,1},{9... | collective-permute-start | bytes 786440 | tf_op jit(solution)/shard_map/ppermute | solution.py:30
  14.6 1.3 collective-permute-start
  15.9 1.3 collective-permute-start.1
  19.5 4.6 %collective-permute-start.11 = (bf16[8,16,512]{2,1,0:T(8,128)(2,1)S(1)}, bf16[8,16,512]{2,1,0:T(8,128)(2,1)S(1)}, u32[]{:S(2)}, u32[]{:S(2)}) collective-permute-start(bf16[8,16,512]{2,1,0:T(8,128)(2,1)S(1)} %get-tuple-element.79), channel_id=1, source_target_pairs={{0,4},{4,8},{8,12},{12,16},{16,20},{20,24},{24,28},{1,5},{5,9},{9,... | collective-permute-start | bytes 393224 | tf_op jit(solution)/shard_map/ppermute | solution.py:42
  25.1 3.3 %collective-permute-done = bf16[8,16,512]{2,1,0:T(8,128)(2,1)S(1)} collective-permute-done((bf16[8,16,512]{2,1,0:T(8,128)(2,1)S(1)}, bf16[8,16,512]{2,1,0:T(8,128)(2,1)S(1)}, u32[]{:S(2)}, u32[]{:S(2)}) %collective-permute-start) | collective-permute-done | bytes 131104 | tf_op jit(solution)/shard_map/ppermute | solution.py:42
  29.8 1.3 collective-permute-start.2
  31.1 1.3 collective-permute-start.3
  32.4 3.3 %collective-permute-done.12 = bf16[8,16,512]{2,1,0:T(8,128)(2,1)S(1)} collective-permute-done((bf16[8,16,512]{2,1,0:T(8,128)(2,1)S(1)}, bf16[8,16,512]{2,1,0:T(8,128)(2,1)S(1)}, u32[]{:S(2)}, u32[]{:S(2)}) %collective-permute-start.12) | collective-permute-done | bytes 131104 | tf_op jit(solution)/shard_map/ppermute | solution.py:45
  35.8 1.5 collective-permute-start.13
  37.3 1.3 collective-permute-start.14
  38.7 3.2 %collective-permute-start.5 = (bf16[4,64,512]{2,1,0:T(8,128)(2,1)S(1)}, bf16[4,64,512]{2,1,0:T(8,128)(2,1)S(1)}, u32[]{:S(2)}, u32[]{:S(2)}) collective-permute-start(bf16[4,64,512]{2,1,0:T(8,128)(2,1)S(1)} %collective-permute-done.4), channel_id=1, source_target_pairs={{0,4},{4,8},{8,12},{12,16},{16,20},{20,24},{24,28},{28,0},{1,5},{5... | collective-permute-start | bytes 786440 | tf_op jit(solution)/shard_map/ppermute | solution.py:28
  41.8 1.9 collective-permute-start.9
  45.5 1.5 slice_bitcast_fusion
  50.4 1.5 fusion.451
  51.9 3.2 %collective-permute-start.6 = (bf16[4,64,512]{2,1,0:T(8,128)(2,1)S(1)}, bf16[4,64,512]{2,1,0:T(8,128)(2,1)S(1)}, u32[]{:S(2)}, u32[]{:S(2)}) collective-permute-start(bf16[4,64,512]{2,1,0:T(8,128)(2,1)S(1)} %collective-permute-done.5), channel_id=1, source_target_pairs={{0,4},{4,8},{8,12},{12,16},{16,20},{20,24},{24,28},{28,0},{1,5},{5... | collective-permute-start | bytes 786440 | tf_op jit(solution)/shard_map/ppermute | solution.py:28
  55.1 1.5 fusion.453
  56.6 1.5 fusion.454
  58.1 6.0 %collective-permute-done.6 = bf16[4,64,512]{2,1,0:T(8,128)(2,1)S(1)} collective-permute-done((bf16[4,64,512]{2,1,0:T(8,128)(2,1)S(1)}, bf16[4,64,512]{2,1,0:T(8,128)(2,1)S(1)}, u32[]{:S(2)}, u32[]{:S(2)}) %collective-permute-start.6) | collective-permute-done | bytes 262176 | tf_op jit(solution)/shard_map/ppermute | solution.py:28
  64.1 1.5 fusion.456
  66.5 4.7 %collective-permute-start.10 = (bf16[4,64,512]{2,1,0:T(8,128)(2,1)S(1)}, bf16[4,64,512]{2,1,0:T(8,128)(2,1)S(1)}, u32[]{:S(2)}, u32[]{:S(2)}) collective-permute-start(bf16[4,64,512]{2,1,0:T(8,128)(2,1)S(1)} %collective-permute-done.9), channel_id=1, source_target_pairs={{4,0},{8,4},{12,8},{16,12},{20,16},{24,20},{28,24},{0,28},{5,1},{9... | collective-permute-start | bytes 786440 | tf_op jit(solution)/shard_map/ppermute | solution.py:30
  71.2 5.2 %collective-permute-done.7 = bf16[4,64,512]{2,1,0:T(8,128)(2,1)S(1)} collective-permute-done((bf16[4,64,512]{2,1,0:T(8,128)(2,1)S(1)}, bf16[4,64,512]{2,1,0:T(8,128)(2,1)S(1)}, u32[]{:S(2)}, u32[]{:S(2)}) %collective-permute-start.7) | collective-permute-done | bytes 262176 | tf_op jit(solution)/shard_map/ppermute | solution.py:28
  82.3 2.3 gather_fusion
  84.6 1.4 gather_fusion.1
  94.7 2.1 fusion.84
  96.8 2.2 convolution_add_fusion.24
  99.0 2.2 convolution_add_fusion.23
  101.3 1.4 convolution_add_fusion.22
  102.7 1.3 convolution_add_fusion.21
  104.1 1.3 convolution_add_fusion.20
  105.4 1.3 convolution_add_fusion.19
  108.6 4.5 %collective-permute-start.15 = (f32[8,16,4]{1,0,2:T(8,128)S(1)}, f32[8,16,4]{1,0,2:T(8,128)S(1)}, u32[]{:S(2)}, u32[]{:S(2)}) collective-permute-start(f32[8,16,4]{1,0,2:T(8,128)S(1)} %slice.401), channel_id=1, source_target_pairs={{0,4},{4,8},{8,12},{12,16},{16,20},{20,24},{24,28},{1,5},{5,9},{9,... | collective-permute-start | bytes 6152 | tf_op jit(solution)/shard_map/ppermute | solution.py:42
  115.9 4.0 %collective-permute-done.16 = f32[8,16,4]{1,0,2:T(8,128)S(1)} collective-permute-done((f32[8,16,4]{1,0,2:T(8,128)S(1)}, f32[8,16,4]{1,0,2:T(8,128)S(1)}, u32[]{:S(2)}, u32[]{:S(2)}) %collective-permute-start.16) | collective-permute-done | bytes 2080 | tf_op jit(solution)/shard_map/ppermute | solution.py:45
  120.0 1.3 collective-permute-start.17
  121.3 1.5 collective-permute-start.18
  130.4 2.0 convolution_add_fusion.15
  132.3 2.2 convolution_add_fusion.14
  134.5 2.1 convolution_add_fusion.13
  136.6 2.1 convolution_add_fusion.12
  138.7 2.0 convolution_add_fusion.11
  140.7 2.0 convolution_add_fusion.10
  142.8 2.0 convolution_add_fusion.9
  144.8 2.0 fusion.81
  156.6 129.6 %all-reduce.3.cloned.1.call-done = (f32[256,256]{0,1:T(8,128)}, f32[256,256]{0,1:T(8,128)}, f32[256,256]{0,1:T(8,128)}, f32[256,256]{1,0:T(8,128)}) async-done(((f32[256,256]{0,1:T(8,128)}, f32[256,256]{0,1:T(8,128)}, f32[256,256]{0,1:T(8,128)}, f32[256,256]{1,0:T(8,128)}), (f32[256,256]{0,1:T(8,128)}, f32[256,256]{0,1:T(8,128)}, f32[256,256]{0,1:T(8,128)}, ...) | async-done | bytes 1048592 | tf_op jit(solution)/shard_map/psum | solution.py:267
  286.2 1.8 copy.347
  288.0 1.8 copy.348
  289.8 1.8 copy.349
  291.6 1.7 copy.932
  (308 shorter events, 47.4 us)
Async XLA Ops:
  7.2 16.9 %copy-start.66 = (s32[1,1,4,2]{2,3,1,0:T(2,128)S(1)}, s32[1,1,4,2]{2,3,1,0:T(2,128)}, u32[]{:S(2)}) copy-start(s32[1,1,4,2]{2,3,1,0:T(2,128)} %param.15) | copy-start | bytes 100
  7.2 16.9 %copy-start.65 = (s32[1,1,4,2]{2,3,1,0:T(2,128)S(1)}, s32[1,1,4,2]{2,3,1,0:T(2,128)}, u32[]{:S(2)}) copy-start(s32[1,1,4,2]{2,3,1,0:T(2,128)} %param.16) | copy-start | bytes 100
  7.2 279.0 %all-reduce.3.cloned.1.call-start = ((), (), s32[]{:S(2)}) async-start(), calls=%async_computation | async-start | bytes 2097152 | tf_op jit(solution)/shard_map/psum | solution.py:267
  7.2 30.1 %collective-permute-start.4 = (bf16[4,64,512]{2,1,0:T(8,128)(2,1)}, bf16[4,64,512]{2,1,0:T(8,128)(2,1)S(1)}, u32[]{:S(2)}, u32[]{:S(2)}) collective-permute-start(bf16[4,64,512]{2,1,0:T(8,128)(2,1)} %bitcast.516), channel_id=1, source_target_pairs={{0,4},{4,8},{8,12},{12,16},{16,20},{20,24},{24,28},{28,0},{1,5},{5... | collective-permute-start | bytes 786440 | tf_op jit(solution)/shard_map/ppermute | solution.py:28
  10.2 28.4 %collective-permute-start.8 = (bf16[4,64,512]{2,1,0:T(8,128)(2,1)}, bf16[4,64,512]{2,1,0:T(8,128)(2,1)S(1)}, u32[]{:S(2)}, u32[]{:S(2)}) collective-permute-start(bf16[4,64,512]{2,1,0:T(8,128)(2,1)} %bitcast.517), channel_id=1, source_target_pairs={{4,0},{8,4},{12,8},{16,12},{20,16},{24,20},{28,24},{0,28},{5,1},{9... | collective-permute-start | bytes 786440 | tf_op jit(solution)/shard_map/ppermute | solution.py:30
  14.6 13.8 %collective-permute-start = (bf16[8,16,512]{2,1,0:T(8,128)(2,1)S(1)}, bf16[8,16,512]{2,1,0:T(8,128)(2,1)S(1)}, u32[]{:S(2)}, u32[]{:S(2)}) collective-permute-start(bf16[8,16,512]{2,1,0:T(8,128)(2,1)S(1)} %bitcast.523), channel_id=1, source_target_pairs={{0,4},{4,8},{8,12},{12,16},{16,20},{20,24},{24,28},{1,5},{5,9},{9,... | collective-permute-start | bytes 393224 | tf_op jit(solution)/shard_map/ppermute | solution.py:42
  15.9 13.8 %collective-permute-start.1 = (bf16[8,16,512]{2,1,0:T(8,128)(2,1)S(1)}, bf16[8,16,512]{2,1,0:T(8,128)(2,1)S(1)}, u32[]{:S(2)}, u32[]{:S(2)}) collective-permute-start(bf16[8,16,512]{2,1,0:T(8,128)(2,1)S(1)} %bitcast.522), channel_id=1, source_target_pairs={{4,0},{8,4},{12,8},{16,12},{20,16},{24,20},{28,24},{5,1},{9,5},{13... | collective-permute-start | bytes 393224 | tf_op jit(solution)/shard_map/ppermute | solution.py:45
  19.5 11.6 %collective-permute-start.11 = (bf16[8,16,512]{2,1,0:T(8,128)(2,1)S(1)}, bf16[8,16,512]{2,1,0:T(8,128)(2,1)S(1)}, u32[]{:S(2)}, u32[]{:S(2)}) collective-permute-start(bf16[8,16,512]{2,1,0:T(8,128)(2,1)S(1)} %get-tuple-element.79), channel_id=1, source_target_pairs={{0,4},{4,8},{8,12},{12,16},{16,20},{20,24},{24,28},{1,5},{5,9},{9,... | collective-permute-start | bytes 393224 | tf_op jit(solution)/shard_map/ppermute | solution.py:42
  24.4 22.5 %copy-start.73 = (pred[2,2]{1,0:T(4,128)(4,1)}, pred[2,2]{1,0:T(4,128)(4,1)S(1)}, u32[]{:S(2)}) copy-start(pred[2,2]{1,0:T(4,128)(4,1)S(1)} %get-tuple-element.110) | copy-start | bytes 16
  24.4 23.5 %copy-start.67 = (pred[2,2]{1,0:T(4,128)(4,1)}, pred[2,2]{1,0:T(4,128)(4,1)S(1)}, u32[]{:S(2)}) copy-start(pred[2,2]{1,0:T(4,128)(4,1)S(1)} %get-tuple-element.106) | copy-start | bytes 16
  24.5 24.3 %copy-start.69 = (pred[2,2]{1,0:T(4,128)(4,1)}, pred[2,2]{1,0:T(4,128)(4,1)S(1)}, u32[]{:S(2)}) copy-start(pred[2,2]{1,0:T(4,128)(4,1)S(1)} %get-tuple-element.107) | copy-start | bytes 16
  24.5 25.1 %copy-start.71 = (pred[2,2]{1,0:T(4,128)(4,1)}, pred[2,2]{1,0:T(4,128)(4,1)S(1)}, u32[]{:S(2)}) copy-start(pred[2,2]{1,0:T(4,128)(4,1)S(1)} %get-tuple-element.108) | copy-start | bytes 16
  24.5 25.9 %copy-start.72 = (pred[2,2]{1,0:T(4,128)(4,1)}, pred[2,2]{1,0:T(4,128)(4,1)S(1)}, u32[]{:S(2)}) copy-start(pred[2,2]{1,0:T(4,128)(4,1)S(1)} %get-tuple-element.109) | copy-start | bytes 16
  24.5 30.6 %copy-start.75 = (pred[2,2]{1,0:T(4,128)(4,1)}, pred[2,2]{1,0:T(4,128)(4,1)S(1)}, u32[]{:S(2)}) copy-start(pred[2,2]{1,0:T(4,128)(4,1)S(1)} %get-tuple-element.111) | copy-start | bytes 16
  24.5 32.1 %copy-start.77 = (pred[2,2]{1,0:T(4,128)(4,1)}, pred[2,2]{1,0:T(4,128)(4,1)S(1)}, u32[]{:S(2)}) copy-start(pred[2,2]{1,0:T(4,128)(4,1)S(1)} %get-tuple-element.112) | copy-start | bytes 16
  24.5 39.6 %copy-start.79 = (pred[2,2]{1,0:T(4,128)(4,1)}, pred[2,2]{1,0:T(4,128)(4,1)S(1)}, u32[]{:S(2)}) copy-start(pred[2,2]{1,0:T(4,128)(4,1)S(1)} %get-tuple-element.105) | copy-start | bytes 16
  24.5 41.1 %copy-start.81 = (pred[2,2]{1,0:T(4,128)(4,1)}, pred[2,2]{1,0:T(4,128)(4,1)S(1)}, u32[]{:S(2)}) copy-start(pred[2,2]{1,0:T(4,128)(4,1)S(1)} %get-tuple-element.113) | copy-start | bytes 16
  24.7 40.9 %copy-start.49 = (bf16[2,2,64,2,128]{4,3,2,1,0:T(2,128)(2,1)}, bf16[2,2,64,2,128]{4,3,2,1,0:T(2,128)(2,1)S(1)}, u32[]{:S(2)}) copy-start(bf16[2,2,64,2,128]{4,3,2,1,0:T(2,128)(2,1)S(1)} %reshape_reshape.29) | copy-start | bytes 393220
  28.4 7.3 %collective-permute-start.12 = (bf16[8,16,512]{2,1,0:T(8,128)(2,1)S(1)}, bf16[8,16,512]{2,1,0:T(8,128)(2,1)S(1)}, u32[]{:S(2)}, u32[]{:S(2)}) collective-permute-start(bf16[8,16,512]{2,1,0:T(8,128)(2,1)S(1)} %get-tuple-element.80), channel_id=1, source_target_pairs={{4,0},{8,4},{12,8},{16,12},{20,16},{24,20},{28,24},{5,1},{9,5},{13... | collective-permute-start | bytes 393224 | tf_op jit(solution)/shard_map/ppermute | solution.py:45
  29.8 12.0 %collective-permute-start.2 = (bf16[32,8,512]{2,1,0:T(8,128)(2,1)S(1)}, bf16[32,8,512]{2,1,0:T(8,128)(2,1)S(1)}, u32[]{:S(2)}, u32[]{:S(2)}) collective-permute-start(bf16[32,8,512]{2,1,0:T(8,128)(2,1)S(1)} %get-tuple-element.77), channel_id=1, source_target_pairs={{0,1},{1,2},{2,3},{4,5},{5,6},{6,7},{8,9},{9,10},{10,11},{12,13},{... | collective-permute-start | bytes 786440 | tf_op jit(solution)/shard_map/ppermute | solution.py:42
  31.1 12.6 %collective-permute-start.3 = (bf16[32,8,512]{2,1,0:T(8,128)(2,1)S(1)}, bf16[32,8,512]{2,1,0:T(8,128)(2,1)S(1)}, u32[]{:S(2)}, u32[]{:S(2)}) collective-permute-start(bf16[32,8,512]{2,1,0:T(8,128)(2,1)S(1)} %get-tuple-element.78), channel_id=1, source_target_pairs={{1,0},{2,1},{3,2},{5,4},{6,5},{7,6},{9,8},{10,9},{11,10},{13,12},{... | collective-permute-start | bytes 786440 | tf_op jit(solution)/shard_map/ppermute | solution.py:45
  35.8 9.4 %collective-permute-start.13 = (bf16[32,8,512]{2,1,0:T(8,128)(2,1)S(1)}, bf16[32,8,512]{2,1,0:T(8,128)(2,1)S(1)}, u32[]{:S(2)}, u32[]{:S(2)}) collective-permute-start(bf16[32,8,512]{2,1,0:T(8,128)(2,1)S(1)} %get-tuple-element.73), channel_id=1, source_target_pairs={{0,1},{1,2},{2,3},{4,5},{5,6},{6,7},{8,9},{9,10},{10,11},{12,13},{... | collective-permute-start | bytes 786440 | tf_op jit(solution)/shard_map/ppermute | solution.py:42
  37.3 7.9 %collective-permute-start.14 = (bf16[32,8,512]{2,1,0:T(8,128)(2,1)S(1)}, bf16[32,8,512]{2,1,0:T(8,128)(2,1)S(1)}, u32[]{:S(2)}, u32[]{:S(2)}) collective-permute-start(bf16[32,8,512]{2,1,0:T(8,128)(2,1)S(1)} %get-tuple-element.74), channel_id=1, source_target_pairs={{1,0},{2,1},{3,2},{5,4},{6,5},{7,6},{9,8},{10,9},{11,10},{13,12},{... | collective-permute-start | bytes 786440 | tf_op jit(solution)/shard_map/ppermute | solution.py:45
  38.7 13.2 %collective-permute-start.5 = (bf16[4,64,512]{2,1,0:T(8,128)(2,1)S(1)}, bf16[4,64,512]{2,1,0:T(8,128)(2,1)S(1)}, u32[]{:S(2)}, u32[]{:S(2)}) collective-permute-start(bf16[4,64,512]{2,1,0:T(8,128)(2,1)S(1)} %collective-permute-done.4), channel_id=1, source_target_pairs={{0,4},{4,8},{8,12},{12,16},{16,20},{20,24},{24,28},{28,0},{1,5},{5... | collective-permute-start | bytes 786440 | tf_op jit(solution)/shard_map/ppermute | solution.py:28
  41.8 24.6 %collective-permute-start.9 = (bf16[4,64,512]{2,1,0:T(8,128)(2,1)S(1)}, bf16[4,64,512]{2,1,0:T(8,128)(2,1)S(1)}, u32[]{:S(2)}, u32[]{:S(2)}) collective-permute-start(bf16[4,64,512]{2,1,0:T(8,128)(2,1)S(1)} %collective-permute-done.8), channel_id=1, source_target_pairs={{4,0},{8,4},{12,8},{16,12},{20,16},{24,20},{28,24},{0,28},{5,1},{9... | collective-permute-start | bytes 786440 | tf_op jit(solution)/shard_map/ppermute | solution.py:30
  45.2 9.9 %copy-start.45 = (bf16[2,2,8,2,8,128]{5,4,3,2,1,0:T(8,128)(2,1)}, bf16[2,2,8,2,8,128]{5,4,3,2,1,0:T(8,128)(2,1)S(1)}, u32[]{:S(2)}) copy-start(bf16[2,2,8,2,8,128]{5,4,3,2,1,0:T(8,128)(2,1)S(1)} %get-tuple-element.68) | copy-start | bytes 393220
  45.2 11.4 %copy-start.46 = (bf16[2,2,8,2,8,128]{5,4,3,2,1,0:T(8,128)(2,1)}, bf16[2,2,8,2,8,128]{5,4,3,2,1,0:T(8,128)(2,1)S(1)}, u32[]{:S(2)}) copy-start(bf16[2,2,8,2,8,128]{5,4,3,2,1,0:T(8,128)(2,1)S(1)} %get-tuple-element.69) | copy-start | bytes 393220
  45.2 18.9 %copy-start.47 = (bf16[2,2,8,2,8,128]{5,4,3,2,1,0:T(8,128)(2,1)}, bf16[2,2,8,2,8,128]{5,4,3,2,1,0:T(8,128)(2,1)S(1)}, u32[]{:S(2)}) copy-start(bf16[2,2,8,2,8,128]{5,4,3,2,1,0:T(8,128)(2,1)S(1)} %get-tuple-element.70) | copy-start | bytes 393220
  45.2 20.4 %copy-start.48 = (bf16[2,2,8,2,8,128]{5,4,3,2,1,0:T(8,128)(2,1)}, bf16[2,2,8,2,8,128]{5,4,3,2,1,0:T(8,128)(2,1)S(1)}, u32[]{:S(2)}) copy-start(bf16[2,2,8,2,8,128]{5,4,3,2,1,0:T(8,128)(2,1)S(1)} %get-tuple-element.71) | copy-start | bytes 393220
  51.9 12.2 %collective-permute-start.6 = (bf16[4,64,512]{2,1,0:T(8,128)(2,1)S(1)}, bf16[4,64,512]{2,1,0:T(8,128)(2,1)S(1)}, u32[]{:S(2)}, u32[]{:S(2)}) collective-permute-start(bf16[4,64,512]{2,1,0:T(8,128)(2,1)S(1)} %collective-permute-done.5), channel_id=1, source_target_pairs={{0,4},{4,8},{8,12},{12,16},{16,20},{20,24},{24,28},{28,0},{1,5},{5... | collective-permute-start | bytes 786440 | tf_op jit(solution)/shard_map/ppermute | solution.py:28
  55.1 24.3 %copy-start.58 = (bf16[1,1,4,64,512]{4,3,2,1,0:T(8,128)(2,1)S(1)}, bf16[1,1,4,64,512]{4,3,2,1,0:T(8,128)(2,1)}, u32[]{:S(2)}) copy-start(bf16[1,1,4,64,512]{4,3,2,1,0:T(8,128)(2,1)} %param.14) | copy-start | bytes 786436
  64.1 12.3 %collective-permute-start.7 = (bf16[4,64,512]{2,1,0:T(8,128)(2,1)S(1)}, bf16[4,64,512]{2,1,0:T(8,128)(2,1)S(1)}, u32[]{:S(2)}, u32[]{:S(2)}) collective-permute-start(bf16[4,64,512]{2,1,0:T(8,128)(2,1)S(1)} %collective-permute-done.6), channel_id=1, source_target_pairs={{0,4},{4,8},{8,12},{12,16},{16,20},{20,24},{24,28},{28,0},{1,5},{5... | collective-permute-start | bytes 786440 | tf_op jit(solution)/shard_map/ppermute | solution.py:28
  66.5 15.1 %collective-permute-start.10 = (bf16[4,64,512]{2,1,0:T(8,128)(2,1)S(1)}, bf16[4,64,512]{2,1,0:T(8,128)(2,1)S(1)}, u32[]{:S(2)}, u32[]{:S(2)}) collective-permute-start(bf16[4,64,512]{2,1,0:T(8,128)(2,1)S(1)} %collective-permute-done.9), channel_id=1, source_target_pairs={{4,0},{8,4},{12,8},{16,12},{20,16},{24,20},{28,24},{0,28},{5,1},{9... | collective-permute-start | bytes 786440 | tf_op jit(solution)/shard_map/ppermute | solution.py:30
  107.2 8.4 %copy-start.57 = (bf16[2,2,64,2,128]{4,2,3,1,0:T(8,128)(2,1)S(1)}, bf16[2,2,64,2,128]{4,2,3,1,0:T(8,128)(2,1)}, u32[]{:S(2)}) copy-start(bf16[2,2,64,2,128]{4,2,3,1,0:T(8,128)(2,1)} %get-tuple-element.135) | copy-start | bytes 393220
  107.6 15.1 %copy-start.51 = (bf16[16,16,256]{2,1,0:T(8,128)(2,1)S(1)}, bf16[16,16,256]{2,1,0:T(8,128)(2,1)}, u32[]{:S(2)}) copy-start(bf16[16,16,256]{2,1,0:T(8,128)(2,1)} %param.17) | copy-start | bytes 393220
  108.3 7.3 %copy-start.52 = (bf16[2,8,2,8,256]{4,3,2,1,0:T(8,128)(2,1)}, bf16[2,8,2,8,256]{4,3,2,1,0:T(8,128)(2,1)S(1)}, u32[]{:S(2)}) copy-start(bf16[2,8,2,8,256]{4,3,2,1,0:T(8,128)(2,1)S(1)} %copy.265) | copy-start | bytes 393220
  108.4 17.1 %copy-start.30 = (bf16[2,2,8,2,8,128]{5,4,3,2,1,0:T(8,128)(2,1)S(1)}, bf16[2,2,8,2,8,128]{5,4,3,2,1,0:T(8,128)(2,1)}, u32[]{:S(2)}) copy-start(bf16[2,2,8,2,8,128]{5,4,3,2,1,0:T(8,128)(2,1)} %copy-done.29) | copy-start | bytes 393220
  108.5 17.1 %copy-start.38 = (bf16[2,2,8,2,8,128]{5,4,3,2,1,0:T(8,128)(2,1)S(1)}, bf16[2,2,8,2,8,128]{5,4,3,2,1,0:T(8,128)(2,1)}, u32[]{:S(2)}) copy-start(bf16[2,2,8,2,8,128]{5,4,3,2,1,0:T(8,128)(2,1)} %get-tuple-element.54) | copy-start | bytes 393220
  108.5 17.1 %copy-start.82 = (pred[2,2]{1,0:T(4,128)(4,1)S(1)}, pred[2,2]{1,0:T(4,128)(4,1)}, u32[]{:S(2)}) copy-start(pred[2,2]{1,0:T(4,128)(4,1)} %copy-done.81) | copy-start | bytes 16
  108.6 7.3 %collective-permute-start.15 = (f32[8,16,4]{1,0,2:T(8,128)S(1)}, f32[8,16,4]{1,0,2:T(8,128)S(1)}, u32[]{:S(2)}, u32[]{:S(2)}) collective-permute-start(f32[8,16,4]{1,0,2:T(8,128)S(1)} %slice.401), channel_id=1, source_target_pairs={{0,4},{4,8},{8,12},{12,16},{16,20},{20,24},{24,28},{1,5},{5,9},{9,... | collective-permute-start | bytes 6152 | tf_op jit(solution)/shard_map/ppermute | solution.py:42
  114.0 11.8 %copy-start.13 = (bf16[2,2,8,2,8,128]{5,4,3,2,1,0:T(8,128)(2,1)S(1)}, bf16[2,2,8,2,8,128]{5,4,3,2,1,0:T(8,128)(2,1)}, u32[]{:S(2)}) copy-start(bf16[2,2,8,2,8,128]{5,4,3,2,1,0:T(8,128)(2,1)} %get-tuple-element.53) | copy-start | bytes 393220
  114.3 5.6 %collective-permute-start.16 = (f32[8,16,4]{1,0,2:T(8,128)S(1)}, f32[8,16,4]{1,0,2:T(8,128)S(1)}, u32[]{:S(2)}, u32[]{:S(2)}) collective-permute-start(f32[8,16,4]{1,0,2:T(8,128)S(1)} %slice.403), channel_id=1, source_target_pairs={{4,0},{8,4},{12,8},{16,12},{20,16},{24,20},{28,24},{5,1},{9,5},{13... | collective-permute-start | bytes 6152 | tf_op jit(solution)/shard_map/ppermute | solution.py:45
  120.0 3.7 %collective-permute-start.17 = (f32[32,8,4]{1,0,2:T(8,128)S(1)}, f32[32,8,4]{1,0,2:T(8,128)S(1)}, u32[]{:S(2)}, u32[]{:S(2)}) collective-permute-start(f32[32,8,4]{1,0,2:T(8,128)S(1)} %get-tuple-element.83), channel_id=1, source_target_pairs={{0,1},{1,2},{2,3},{4,5},{5,6},{6,7},{8,9},{9,10},{10,11},{12,13},{... | collective-permute-start | bytes 12296 | tf_op jit(solution)/shard_map/ppermute | solution.py:42
  121.3 3.1 %collective-permute-start.18 = (f32[32,8,4]{1,0,2:T(8,128)S(1)}, f32[32,8,4]{1,0,2:T(8,128)S(1)}, u32[]{:S(2)}, u32[]{:S(2)}) collective-permute-start(f32[32,8,4]{1,0,2:T(8,128)S(1)} %get-tuple-element.84), channel_id=1, source_target_pairs={{1,0},{2,1},{3,2},{5,4},{6,5},{7,6},{9,8},{10,9},{11,10},{13,12},{... | collective-permute-start | bytes 12296 | tf_op jit(solution)/shard_map/ppermute | solution.py:45
  130.4 8.3 %copy-start.8 = (bf16[2,2,8,2,8,128]{5,4,3,2,1,0:T(8,128)(2,1)S(1)}, bf16[2,2,8,2,8,128]{5,4,3,2,1,0:T(8,128)(2,1)}, u32[]{:S(2)}) copy-start(bf16[2,2,8,2,8,128]{5,4,3,2,1,0:T(8,128)(2,1)} %get-tuple-element.43) | copy-start | bytes 393220
  132.3 8.4 %copy-start.7 = (bf16[2,2,8,2,8,128]{5,4,3,2,1,0:T(8,128)(2,1)S(1)}, bf16[2,2,8,2,8,128]{5,4,3,2,1,0:T(8,128)(2,1)}, u32[]{:S(2)}) copy-start(bf16[2,2,8,2,8,128]{5,4,3,2,1,0:T(8,128)(2,1)} %get-tuple-element.41) | copy-start | bytes 393220
  134.5 8.3 %copy-start.6 = (bf16[2,2,8,2,8,128]{5,4,3,2,1,0:T(8,128)(2,1)S(1)}, bf16[2,2,8,2,8,128]{5,4,3,2,1,0:T(8,128)(2,1)}, u32[]{:S(2)}) copy-start(bf16[2,2,8,2,8,128]{5,4,3,2,1,0:T(8,128)(2,1)} %get-tuple-element.39) | copy-start | bytes 393220
  136.6 8.2 %copy-start.27 = (bf16[2,2,8,2,8,128]{5,4,3,2,1,0:T(8,128)(2,1)S(1)}, bf16[2,2,8,2,8,128]{5,4,3,2,1,0:T(8,128)(2,1)}, u32[]{:S(2)}) copy-start(bf16[2,2,8,2,8,128]{5,4,3,2,1,0:T(8,128)(2,1)} %get-tuple-element.37) | copy-start | bytes 393220
  (55 other events, 178.6 us)
Sparse Core Ops, SparseCore 0:
  154.8 131.3 all-reduce.2
